TPU v7x, 32 devices: a whole 2x2x4 slice. The times are simulated.
32 devices in a mesh: seq: 8 (over z, y), mp: 4 (over x, core).
Axes of the slice: x: 2, y: 2, z: 4, core: 2. Of those that a mesh axis runs over, the one named last changes fastest.
Arguments:
- query: bfloat16 [3840, 5120], P('seq', 'mp'), may hold values from -32 to 32
- query_gain: float32 [5120], P('mp'), may hold values from 0.25 to 1.75
- cond: bfloat16 [8, 2, 128, 5120], P('seq', None, None, 'mp'), may hold values from -32 to 32
- key_gain: float32 [5120], P('mp'), may hold values from 0.25 to 1.75
- grad_out: bfloat16 [3840, 5120], P('seq', 'mp'), may hold values from -15 to 15
- clip_len: int32 [3], replicated, may hold values from 1 to 1920, 3840 in all
- clip_owner: int32 [3], replicated, may hold values from 0 to 7, as said below
Outputs:
- grad_query: bfloat16 [3840, 5120], P('seq', 'mp')
- grad_cond: bfloat16 [8, 2, 128, 5120], P('seq', None, None, 'mp')
Inputs may be any that keep to these rules, and one draw needn't show every extreme that they name: `clip_len`: the clip lengths sum to 3840, and the longest is exactly 1920. `clip_owner`: the owners of the 3 clips are distinct slots.
All inputs are finite; a program needn't handle non-finite values.
Results may differ from a plain program's by a relative error of at most 0.011.
Values may be sent and summed in bfloat16 or wider, within the bound.
No kernel may reach another device: no remote copies, remote signals or barrier semaphores. Data moves between devices by JAX's collectives and lax.ppermute only.
A program may use at most 128 MiB of HBM per device.

v0:
```python
import math
import jax
import jax.numpy as jnp
from jax import lax
from jax.sharding import PartitionSpec as P

D = 5120
HEAD_DIM = 128
EPS = 1e-06
MASKED = -1e30


def broadcast(value, axis, root):
    mine = lax.axis_index(axis) == root
    return lax.psum(jnp.where(mine, value, jnp.zeros_like(value)), axis)


def attend(query_heads, key_heads, value_heads, grad_heads, allowed, score_scale):
    scores = (
        jnp.einsum("thd,khd->htk", query_heads, key_heads, preferred_element_type=jnp.float32)
        * score_scale
    )
    scores = jnp.where(allowed[None, :, :], scores, MASKED)
    row_max = jnp.max(scores, axis=2, keepdims=True)
    weights = jnp.exp(scores - row_max)
    normed_weights = weights / jnp.sum(weights, axis=2, keepdims=True)
    weights_low = normed_weights.astype(jnp.bfloat16)
    attended = jnp.einsum(
        "htk,khd->thd", weights_low, value_heads, preferred_element_type=jnp.float32
    ).astype(jnp.bfloat16)
    delta = jnp.sum(grad_heads.astype(jnp.float32) * attended.astype(jnp.float32), axis=2)
    grad_weights = jnp.einsum(
        "thd,khd->htk", grad_heads, value_heads, preferred_element_type=jnp.float32
    )
    grad_scores = (
        normed_weights * (grad_weights - jnp.transpose(delta)[:, :, None]) * score_scale
    ).astype(jnp.bfloat16)
    grad_q = jnp.einsum("htk,khd->thd", grad_scores, key_heads, preferred_element_type=jnp.float32)
    grad_k = jnp.einsum(
        "htk,thd->khd", grad_scores, query_heads, preferred_element_type=jnp.float32
    )
    grad_v = jnp.einsum("htk,thd->khd", weights_low, grad_heads, preferred_element_type=jnp.float32)
    return (grad_q, grad_k, grad_v)


def local(query, query_gain, cond, key_gain, grad_out, clip_len, clip_owner):
    tok_rows = query.shape[0]
    feat_width = query.shape[1]
    head_count = feat_width // HEAD_DIM
    clip_count = clip_len.shape[0]
    cond_depth = cond.shape[2]
    my_index = lax.axis_index("seq")
    first_pos = my_index * tok_rows
    position = first_pos + jnp.arange(tok_rows, dtype=jnp.int32)
    starts = jnp.cumsum(clip_len) - clip_len
    clip_of = jnp.sum((position[:, None] >= starts[None, :]).astype(jnp.int32), axis=1) - 1
    query_wide = query.astype(jnp.float32)
    query_sumsq = lax.psum(jnp.sum(query_wide * query_wide, axis=1), "mp")
    query_scale = lax.rsqrt(query_sumsq / D + EPS)
    query_normed = (query_wide * query_scale[:, None] * query_gain).astype(jnp.bfloat16)
    slab_stack = jnp.stack(
        [broadcast(cond[0], "seq", clip_owner[clip_index]) for clip_index in range(clip_count)]
    )
    key_raw = slab_stack[:, 0].astype(jnp.float32)
    key_sumsq = lax.psum(jnp.sum(key_raw * key_raw, axis=2), "mp")
    key_scale = lax.rsqrt(key_sumsq / D + EPS)
    key_normed = (key_raw * key_scale[:, :, None] * key_gain).astype(jnp.bfloat16)
    key_heads = key_normed.reshape(clip_count, cond_depth, head_count, HEAD_DIM)
    value_heads = slab_stack[:, 1].reshape(clip_count, cond_depth, head_count, HEAD_DIM)
    query_heads = query_normed.reshape(tok_rows, head_count, HEAD_DIM)
    grad_heads = grad_out.reshape(tok_rows, head_count, HEAD_DIM)
    score_scale = 1.0 / math.sqrt(HEAD_DIM)
    key_clip = jnp.arange(clip_count * cond_depth, dtype=jnp.int32) // cond_depth
    allowed = clip_of[:, None] == key_clip[None, :]
    grad_query_wide, grad_keys_flat, grad_values_flat = attend(
        query_heads,
        key_heads.reshape(clip_count * cond_depth, head_count, HEAD_DIM),
        value_heads.reshape(clip_count * cond_depth, head_count, HEAD_DIM),
        grad_heads,
        allowed,
        score_scale,
    )
    key_grad = grad_keys_flat.reshape(clip_count, cond_depth, feat_width)
    value_grad = grad_values_flat.reshape(clip_count, cond_depth, feat_width)
    grad_query = grad_query_wide.reshape(tok_rows, feat_width).astype(jnp.bfloat16)
    partial_grads = jnp.stack([key_grad, value_grad], axis=1)
    owner_mask = (clip_owner == my_index).astype(jnp.float32)
    summed = lax.psum(partial_grads, "seq")
    owned_grads = jnp.sum(summed * owner_mask[:, None, None, None], axis=0).astype(jnp.bfloat16)
    return (grad_query, owned_grads[None])


def solution(mesh):
    return jax.shard_map(
        local,
        mesh=mesh,
        in_specs=(
            P("seq", "mp"),
            P("mp"),
            P("seq", None, None, "mp"),
            P("mp"),
            P("seq", "mp"),
            P(),
            P(),
        ),
        out_specs=(P("seq", "mp"), P("seq", None, None, "mp")),
        check_vma=False,
    )
```

profile of v0, /device:TPU:0, one launch (start us, length us, event | category | flops | bytes accessed | tf_op | source)
XLA Modules:
  0.0 390.9 jit_solution(13383794463649991475)
XLA Ops:
  7.2 0.0 all-reduce.7.cloned.1.call-start
  7.2 1.4 fusion.21
  10.6 2.4 broadcast_select_fusion
  13.1 0.0 all-reduce.7.cloned.1.call-update
  13.1 0.0 all-reduce.5.cloned.1.call-start
  13.1 0.0 copy-start.11
  13.1 0.0 copy-start.5
  13.2 1.7 copy.50
  14.8 1.5 copy.53
  16.3 0.0 copy-done.11
  16.3 0.2 reduce-window.9
  16.5 0.1 convert_reduce_fusion
  16.6 0.0 copy-done.5
  16.6 0.3 fusion.8
  16.9 0.2 broadcast_compare_fusion
  17.1 98.0 %all-reduce.7.cloned.1.call-done = (bf16[1,2,128,1280]{3,2,1,0:T(8,128)(2,1)}, bf16[1,2,128,1280]{3,2,1,0:T(8,128)(2,1)}, bf16[1,2,128,1280]{3,2,1,0:T(8,128)(2,1)}) async-done(((bf16[1,2,128,1280]{3,2,1,0:T(8,128)(2,1)}, bf16[1,2,128,1280]{3,2,1,0:T(8,128)(2,1)}, bf16[1,2,128,1280]{3,2,1,0:T(8,128)(2,1)}), (bf16[1,2,128,1280]{3,2,1,0:T(8,128)(2,1)}, bf16[1,2,128,1280]{3,2,1,0:T(8,128)(2,1)}, ...) | async-done | bytes 1966096 | tf_op jit(solution)/shard_map/psum | solution.py:15
  115.1 0.0 copy-start.7
  115.1 1.2 constant_dynamic-update-slice_fusion.2
  116.3 1.1 constant_dynamic-update-slice_fusion.1
  117.4 0.0 copy-done.7
  117.5 0.3 multiply_reduce_fusion.1
  117.7 1.2 fusion.20
  118.9 6.8 %all-reduce = (f32[3,128]{1,0:T(4,128)S(1)}, f32[480]{0:T(512)S(1)}) all-reduce(f32[3,128]{1,0:T(4,128)S(1)} %multiply_reduce_fusion.1, f32[480]{0:T(512)S(1)} %fusion.8), channel_id=1, replica_groups=mesh['seq'=8,'mp'=4] {'mp'}, use_global_device_ids=true, to_apply=%region_4.5 | all-reduce | flops 864 | bytes 6912 | tf_op jit(solution)/shard_map/psum | solution.py:65
  125.7 0.0 copy-start.8
  125.7 3.4 copy.49
  129.1 3.7 reshape_reshape_squeeze.3
  132.8 0.0 copy-done.8
  132.8 2.7 fusion.10
  135.5 2.4 copy.46
  137.9 2.6 copy.45
  140.6 0.0 copy-start.9
  140.6 3.1 reshape.127
  143.6 0.0 copy-start.2
  143.7 0.0 copy-done.9
  143.7 7.8 %fusion.22 = (f32[10,480]{1,0:T(8,128)S(1)}, f32[10,480,384]{2,1,0:T(8,128)}) fusion(pred[480,384]{1,0:T(8,128)(4,1)S(1)} %broadcast_compare_fusion, bf16[480,10,128]{0,2,1:T(8,128)(2,1)} %bitcast.55, f32[384,10,128]{0,2,1:T(8,128)S(1)} %reshape.127, f32[10,128]{1,0:T(8,128)S(1)} %bitcast.58, f32[384]{0:T(512)S(1)} %rsqrt_bitcast_fusion), kind=kOutput, calls=%fused_computation.56 | convolution fusion | flops 480706944 | bytes 10777856 | tf_op jit(solution)/shard_map/sub | solution.py:25
  151.5 0.0 copy-done.2
  151.5 3.6 fusion.7
  155.1 0.0 copy-start.1
  155.1 1.9 copy-done.1
  157.0 1.4 convolution_bitcast_fusion
  158.4 1.8 copy.59
  160.2 0.0 copy-start.6
  160.2 4.0 %fusion.11 = f32[480,10]{0,1:T(8,128)S(1)} fusion(bf16[480,10,128]{2,0,1:T(8,128)(2,1)} %copy.53, bf16[384,10,128]{0,2,1:T(8,128)(2,1)} %reshape_reshape_squeeze.3, bf16[10,480,384]{2,1,0:T(8,128)(2,1)} %copy-done.1), kind=kOutput, calls=%fused_computation.20 | convolution fusion | flops 474926400 | bytes 5917440 | tf_op jit(solution)/shard_map/htk,khd->thd/dot_general | solution.py:28
  164.2 0.0 copy-done.6
  164.2 0.0 copy-start.4
  164.2 4.4 %fusion.2 = bf16[10,480,384]{2,1,0:T(8,128)(2,1)S(1)} fusion(f32[10,480]{1,0:T(8,128)S(1)} %bitcast.61, f32[10,480,384]{2,1,0:T(8,128)} %get-tuple-element.22, f32[10,480]{1,0:T(8,128)S(1)} %get-tuple-element.21, bf16[384,10,128]{0,2,1:T(8,128)(2,1)S(1)} %copy-done.6, bf16[480,10,128]{0,2,1:T(8,128)(2,1)S(1)} %bitcast.53), kind=kOutput, calls=%fused_computation.3 | convolution fusion | flops 481075200 | bytes 13309440 | tf_op jit(solution)/shard_map/thd,khd->htk/dot_general | solution.py:32
  168.6 0.0 copy-start
  168.6 1.9 copy-done
  170.5 0.0 copy-done.4
  170.5 2.1 convolution_bitcast_fusion.1
  172.7 2.7 stack_reshape.6
  175.4 4.0 %stack_reshape.7 = f32[3,1,128,1280]{2,0,3,1:T(4,128)} reshape(f32[384,10,128]{0,2,1:T(8,128)} %copy.59) | data formatting | bytes 3932160 | tf_op jit(solution)/shard_map/stack;reshape | solution.py:86
  179.4 5.0 %pad_maximum_fusion = f32[3,2,128,1280]{2,0,3,1:T(4,128)} fusion(f32[3,1,128,1280]{2,0,3,1:T(4,128)} %stack_reshape.7, f32[3,1,128,1280]{2,0,3,1:T(4,128)S(1)} %stack_reshape.6), kind=kLoop, calls=%fused_computation.7 | loop fusion | flops 983040 | bytes 7864320 | tf_op jit(solution)/shard_map/stack | solution.py:86
  184.5 0.0 copy-start.10
  184.5 0.0 copy-start.3
  184.5 0.0 all-reduce.5.cloned.1.call-update
  184.5 0.6 copy-done.10
  185.1 0.9 copy-done.3
  186.0 3.2 fusion.12
  189.3 0.6 copy.56
  189.9 1.5 copy.60
  191.4 176.1 %all-reduce.5.cloned.1.call-done = f32[3,2,128,1280]{2,0,3,1:T(4,128)} async-done(((f32[3,2,128,1280]{2,0,3,1:T(4,128)}), f32[3,2,128,1280]{2,0,3,1:T(4,128)}) %all-reduce.5.cloned.1.call-update) | async-done | bytes 3932176 | tf_op jit(solution)/shard_map/psum | solution.py:88
  367.5 15.5 %multiply_reduce_fusion = bf16[2,128,1280]{1,2,0:T(8,128)(2,1)S(1)} fusion(f32[3,2,128,1280]{2,0,3,1:T(4,128)} %all-reduce.5.cloned.1.call-done, f32[3]{0:T(128)S(1)} %compare_convert_fusion), kind=kLoop, calls=%fused_computation.8 | loop fusion | flops 1638400 | bytes 4587532 | tf_op jit(solution)/shard_map/reduce_sum | solution.py:89
  383.0 1.1 copy.61
  (8 shorter events, 0.1 us)
Async XLA Ops:
  7.2 107.9 %all-reduce.7.cloned.1.call-start = ((), (), s32[]{:S(2)}) async-start(), calls=%async_computation.1 | async-start | bytes 3932160 | tf_op jit(solution)/shard_map/psum | solution.py:15
  13.1 354.4 %all-reduce.5.cloned.1.call-start = ((), (), s32[]{:S(2)}) async-start(), calls=%async_computation | async-start | bytes 10485760 | tf_op jit(solution)/shard_map/psum | solution.py:88
  13.1 3.2 copy-start.11
  13.1 3.5 copy-start.5
  115.1 2.3 copy-start.7
  125.7 7.1 %copy-start.8 = (f32[1280]{0:T(1024)S(1)}, f32[1280]{0:T(1024)}, u32[]{:S(2)}) copy-start(f32[1280]{0:T(1024)} %param.8) | copy-start | bytes 15364
  140.6 3.1 copy-start.9
  143.6 7.9 %copy-start.2 = (f32[384,10,128]{0,2,1:T(8,128)}, f32[384,10,128]{0,2,1:T(8,128)S(1)}, u32[]{:S(2)}) copy-start(f32[384,10,128]{0,2,1:T(8,128)S(1)} %reshape.127) | copy-start | bytes 5898244
  155.1 1.9 copy-start.1
  160.2 4.0 %copy-start.6 = (bf16[384,10,128]{0,2,1:T(8,128)(2,1)S(1)}, bf16[384,10,128]{0,2,1:T(8,128)(2,1)}, u32[]{:S(2)}) copy-start(bf16[384,10,128]{0,2,1:T(8,128)(2,1)} %reshape_reshape_squeeze.3) | copy-start | bytes 2949124
  164.2 6.3 %copy-start.4 = (bf16[480,1280]{0,1:T(8,128)(2,1)S(1)}, bf16[480,1280]{0,1:T(8,128)(2,1)}, u32[]{:S(2)}) copy-start(bf16[480,1280]{0,1:T(8,128)(2,1)} %copy.46) | copy-start | bytes 3686404
  168.6 1.9 copy-start
  184.5 0.7 copy-start.10
  184.5 1.6 copy-start.3
Sparse Core Ops, SparseCore 0:
  13.2 101.8 all-reduce.6
  184.6 182.7 all-reduce.4
where the time goes:
time: 392 us; the launch traced here: 391 us
  waiting for transfers between devices  274 us (70%)
  local copies, waits for them, and re-layouts  39.3 us (10%)
  other arithmetic  31.4 us (8%)
  matrix products  23 us (6%)
  between operations  16.2 us (4%)
  blocking collectives  6.81 us (2%)
    psum x1, waiting for transfers between devices, local(): summed = lax.psum(partial_grads, 'seq')  176 us
    psum x1, waiting for transfers between devices, broadcast(): return lax.psum(jnp.where(mine, value, jnp.zeros_like(value)), axis)  98 us
    reduce_sum x1, other arithmetic, local(): jnp.sum(summed * owner_mask[:, None, None, None], axis=0)  15.5 us
    unnamed x29, local copies, waits for them, and re-layouts  12 us
    sub x1, matrix products, attend(): weights = jnp.exp(scores - row_max)  7.85 us
  transfers between devices with their start and end apart: 2, of which 2 were waited for; matrix products, arithmetic and copies ran while one was open for 2% of the time, Pallas kernels for 0%

commit v1 on v0

--- a/solution.py
+++ b/solution.py
@@ -85,7 +85,7 @@
     grad_query = grad_query_wide.reshape(tok_rows, feat_width).astype(jnp.bfloat16)
     partial_grads = jnp.stack([key_grad, value_grad], axis=1)
     owner_mask = (clip_owner == my_index).astype(jnp.float32)
-    summed = lax.psum(partial_grads, "seq")
+    summed = jnp.sum(lax.all_gather(partial_grads, "seq"), axis=0)
     owned_grads = jnp.sum(summed * owner_mask[:, None, None, None], axis=0).astype(jnp.bfloat16)
     return (grad_query, owned_grads[None])
 

time: 392 us -> 813 us (2.07)
  waiting for transfers between devices: 274 us -> 688 us
    all_gather x0 -> x1, waiting for transfers between devices: none -> 590 us  [local(): summed = jnp.sum(lax.all_gather(partial_grads, 'seq'), axis=0)]
    psum x1 -> x0, waiting for transfers between devices: 176 us -> none  [local(): summed = lax.psum(partial_grads, 'seq')]
    reduce_sum x0 -> x1, other arithmetic: none -> 13.4 us  [local(): summed = jnp.sum(lax.all_gather(partial_grads, 'seq'), axis=0)]
    reduce_sum x1, other arithmetic: 15.5 us -> 3.52 us  [local(): jnp.sum(summed * owner_mask[:, None, None, None], axis=0)]
  transfers between devices with their start and end apart: 2 -> 2, of which waited for: 2 -> 2; matrix products, arithmetic and copies ran while one was open for 2% -> 1% of each run, Pallas kernels for 0% -> 0%
where the time goes in v1:
time: 813 us; the launch traced here: 812 us
  waiting for transfers between devices  688 us (85%)
  local copies, waits for them, and re-layouts  44.8 us (6%)
  other arithmetic  32.9 us (4%)
  matrix products  23 us (3%)
  between operations  16.2 us (2%)
    all_gather x1, waiting for transfers between devices, local(): summed = jnp.sum(lax.all_gather(partial_grads, 'seq'), axis=0)  590 us
    psum x1, waiting for transfers between devices, broadcast(): return lax.psum(jnp.where(mine, value, jnp.zeros_like(value)), axis)  98 us
  transfers between devices with their start and end apart: 2, of which 2 were waited for; matrix products, arithmetic and copies ran while one was open for 1% of the time, Pallas kernels for 0%

profile of v1, /device:TPU:0, one launch (start us, length us, event | category | flops | bytes accessed | tf_op | source)
XLA Modules:
  0.0 812.4 jit_solution(1122063285126369907)
XLA Ops:
  7.2 0.0 all-reduce.4.cloned.1.call-start
  7.2 1.4 fusion.21
  10.6 2.4 broadcast_select_fusion
  13.1 0.0 all-reduce.4.cloned.1.call-update
  13.1 0.0 all-gather.3.cloned.1.call-start
  13.1 0.0 copy-start.11
  13.1 0.0 copy-start.5
  13.2 1.7 copy.51
  14.8 1.5 copy.54
  16.3 0.0 copy-done.11
  16.3 0.2 reduce-window.9
  16.5 0.1 convert_reduce_fusion
  16.6 0.0 copy-done.5
  16.6 0.3 fusion.8
  16.9 0.2 broadcast_compare_fusion
  17.1 98.0 %all-reduce.4.cloned.1.call-done = (bf16[1,2,128,1280]{3,2,1,0:T(8,128)(2,1)}, bf16[1,2,128,1280]{3,2,1,0:T(8,128)(2,1)}, bf16[1,2,128,1280]{3,2,1,0:T(8,128)(2,1)}) async-done(((bf16[1,2,128,1280]{3,2,1,0:T(8,128)(2,1)}, bf16[1,2,128,1280]{3,2,1,0:T(8,128)(2,1)}, bf16[1,2,128,1280]{3,2,1,0:T(8,128)(2,1)}), (bf16[1,2,128,1280]{3,2,1,0:T(8,128)(2,1)}, bf16[1,2,128,1280]{3,2,1,0:T(8,128)(2,1)}, ...) | async-done | bytes 1966096 | tf_op jit(solution)/shard_map/psum | solution.py:15
  115.1 0.0 copy-start.7
  115.1 1.2 constant_dynamic-update-slice_fusion.2
  116.3 1.1 constant_dynamic-update-slice_fusion.1
  117.4 0.0 copy-done.7
  117.5 0.3 multiply_reduce_fusion.1
  117.7 1.2 fusion.20
  118.9 0.0 copy-start.8
  118.9 6.9 all-reduce
  125.9 3.4 copy.50
  129.3 3.7 reshape_reshape_squeeze.3
  132.9 0.0 copy-done.8
  132.9 2.7 fusion.10
  135.6 2.4 copy.47
  138.0 2.6 copy.46
  140.7 0.0 copy-start.9
  140.7 3.1 reshape.127
  143.8 0.0 copy-start.2
  143.8 0.0 copy-done.9
  143.8 7.8 fusion.22
  151.6 0.0 copy-done.2
  151.6 3.6 fusion.7
  155.2 0.0 copy-start.1
  155.2 1.9 copy-done.1
  157.1 1.4 convolution_bitcast_fusion
  158.5 1.8 copy.60
  160.4 0.0 copy-start.6
  160.4 4.0 fusion.11
  164.4 0.0 copy-done.6
  164.4 0.0 copy-start.4
  164.4 4.4 fusion.2
  168.7 0.0 copy-start
  168.8 1.9 copy-done
  170.6 0.0 copy-done.4
  170.6 2.1 convolution_bitcast_fusion.1
  172.8 2.7 stack_reshape.6
  175.5 4.0 stack_reshape.7
  179.5 5.0 pad_maximum_fusion
  184.6 6.7 copy.61
  191.2 0.0 copy-start.3
  191.2 0.0 all-gather.3.cloned.1.call-update
  191.2 0.6 copy-done.10
  191.9 0.9 copy-done.3
  192.8 3.2 fusion.12
  196.0 0.6 copy.57
  196.6 1.5 copy.62
  198.1 590.5 %all-gather.3.cloned.1.call-done = f32[24,2,128,1280]{3,2,1,0:T(8,128)} async-done(((f32[3,2,128,1280]{3,2,1,0:T(8,128)}), f32[24,2,128,1280]{3,2,1,0:T(8,128)}) %all-gather.3.cloned.1.call-update) | async-done | bytes 31457296 | tf_op jit(solution)/shard_map/all_gather | solution.py:88
  788.6 13.4 %reduce_sum.68 = f32[3,2,128,1280]{3,2,1,0:T(8,128)} reduce(f32[8,3,2,128,1280]{4,3,2,1,0:T(8,128)} %bitcast.52, f32[]{:T(128)} %constant.38.clone.1), dimensions={0}, to_apply=%region_12.13 | reduce | flops 6881280 | bytes 35389444 | tf_op jit(solution)/shard_map/reduce_sum | solution.py:88
  802.0 3.5 multiply_reduce_fusion
  (9 shorter events, 0.1 us)
Async XLA Ops:
  7.2 107.9 %all-reduce.4.cloned.1.call-start = ((), (), s32[]{:S(2)}) async-start(), calls=%async_computation.1 | async-start | bytes 3932160 | tf_op jit(solution)/shard_map/psum | solution.py:15
  13.1 775.5 %all-gather.3.cloned.1.call-start = ((), (), s32[]{:S(2)}) async-start(), calls=%async_computation | async-start | bytes 35389440 | tf_op jit(solution)/shard_map/all_gather | solution.py:88
  13.1 3.2 copy-start.11
  13.1 3.5 copy-start.5
  115.1 2.3 copy-start.7
  118.9 14.0 %copy-start.8 = (f32[1280]{0:T(1024)S(1)}, f32[1280]{0:T(1024)}, u32[]{:S(2)}) copy-start(f32[1280]{0:T(1024)} %param.8) | copy-start | bytes 15364
  140.7 3.1 copy-start.9
  143.8 7.9 copy-start.2
  155.2 1.9 copy-start.1
  160.4 4.0 copy-start.6
  164.4 6.3 copy-start.4
  168.7 1.9 copy-start
  191.2 0.7 copy-start.10
  191.2 1.6 copy-start.3
Sparse Core Ops, SparseCore 0:
  13.2 101.8 all-reduce.3
  191.4 597.1 all-gather.2
